TPU v7x, 128 devices: a whole 4x4x4 slice. The times are simulated.
128 devices in a mesh: leaf: 16 (over z, x), panel: 8 (over y, core).
Axes of the slice: x: 4, y: 4, z: 4, core: 2. Of those that a mesh axis runs over, the one named last changes fastest.
Arguments:
- child_front: float32 [16, 2048, 2048], P('leaf', 'panel'), as said below
- child_panel: bfloat16 [16, 2048, 4096], P('leaf'), may hold values from -0.03125 to 0.03125
- parent_front: float32 [4096, 4096], P('leaf', 'panel'), as said below
- tile_map: int32 [16, 8], P('leaf'), may hold values from 0 to 15, as said below
- tile_count: int32 [16], P('leaf'), may hold values from 2 to 8, as said below
Outputs:
- eliminated: float32 [4096, 4096], P('leaf', 'panel')
Inputs may be any that keep to these rules, and one draw needn't show every extreme that they name: `tile_count`: some child has 8 live tiles and some child has 2. `tile_map`: for child c the first tile_count[c] entries are distinct and rising; the other entries are 0. Each child's block is symmetric, and child_front[c] - child_panel[c] child_panel[c]^T is positive definite. `parent_front`: symmetric positive definite.
All inputs are finite; a program needn't handle non-finite values.
Results may differ from a plain program's by a relative error of at most 0.0003.
Values sent between devices are 32-bit elements; how exact they have to be, the bound alone decides.
No kernel may reach another device: no remote copies, remote signals or barrier semaphores. Data moves between devices by JAX's collectives and lax.ppermute only.
A program may use at most 128 MiB of HBM per device.

v0:
```python
import jax
import jax.numpy as jnp
from jax import lax
from jax.sharding import PartitionSpec as P

TILE = 256
NF = 4096
CB = 2048
STEPS = 4


def spread(array, axis, root):
    mine = lax.axis_index(axis) == root
    return lax.psum(jnp.where(mine, array, jnp.zeros_like(array)), axis)


def finish_rows(block, row_index, factor, pivot_start):
    solved = lax.linalg.triangular_solve(
        factor, block, left_side=False, lower=True, transpose_a=True
    )
    offset = jnp.clip(row_index - pivot_start, 0, TILE - 1)
    own_rows = jnp.take(factor, offset, axis=0)
    inside = (row_index >= pivot_start) & (row_index < pivot_start + TILE)
    kept = jnp.where(inside[:, None], own_rows, solved)
    return jnp.where(row_index[:, None] < pivot_start, 0.0, kept)


def shards(child_front, child_panel, parent_front, tile_map, tile_count):
    highest = lax.Precision.HIGHEST
    panel_count = lax.axis_size("panel")
    leaf_id = lax.axis_index("leaf")
    panel_id = lax.axis_index("panel")
    tiles_child = CB // TILE
    tiles_front = NF // TILE
    pivot_span = STEPS * TILE
    child_rows = child_front.shape[1]
    height = parent_front.shape[0]
    col_width = parent_front.shape[1]
    panel_all = child_panel[0]
    own_panel = lax.dynamic_slice_in_dim(panel_all, panel_id * child_rows, child_rows, 0)
    update = child_front[0] - lax.dot_general(
        own_panel, panel_all, (((1,), (1,)), ((), ())), preferred_element_type=jnp.float32
    )
    mapped = tile_map[0]
    live_tiles = jnp.arange(tiles_child, dtype=jnp.int32) < tile_count[0]
    everywhere = jnp.arange(tiles_front, dtype=jnp.int32)
    chosen = ((mapped[None, :] == everywhere[:, None]) & live_tiles[None, :]).astype(jnp.float32)
    placed = jnp.einsum(
        "rtb,ft->rfb", update.reshape(child_rows, tiles_child, TILE), chosen, precision=highest
    )
    placed = placed.reshape(child_rows, panel_count, col_width)
    moved_cols = lax.all_to_all(placed, "panel", split_axis=1, concat_axis=0, tiled=True)
    column_tiles = moved_cols.reshape(tiles_child, TILE, col_width)
    targets = jnp.arange(lax.axis_size("leaf") * height // TILE, dtype=jnp.int32)
    picked = ((mapped[None, :] == targets[:, None]) & live_tiles[None, :]).astype(jnp.float32)
    front_block = parent_front + lax.psum_scatter(
        jnp.einsum("ft,tbc->fbc", picked, column_tiles, precision=highest).reshape(
            lax.axis_size("leaf") * height, col_width
        ),
        "leaf",
        scatter_dimension=0,
        tiled=True,
    )
    global_rows = leaf_id * height + jnp.arange(height, dtype=jnp.int32)
    global_cols = panel_id * col_width + jnp.arange(col_width, dtype=jnp.int32)
    col_tiles = col_width // TILE
    for pivot_step in range(STEPS):
        source_panel = pivot_step // col_tiles
        local_start = pivot_step % col_tiles * TILE
        pivot_start = pivot_step * TILE
        source = front_block[:, local_start : local_start + TILE]
        column = spread(source, "panel", source_panel)
        full_column = lax.all_gather(column, "leaf", axis=0, tiled=True)
        factor = jnp.linalg.cholesky(full_column[pivot_start : pivot_start + TILE])
        own_factor = finish_rows(column, global_rows, factor, pivot_start)
        col_factor = finish_rows(
            lax.dynamic_slice_in_dim(full_column, panel_id * col_width, col_width, 0),
            global_cols,
            factor,
            pivot_start,
        )
        front_block = front_block - lax.dot_general(
            own_factor,
            col_factor,
            (((1,), (1,)), ((), ())),
            precision=highest,
            preferred_element_type=jnp.float32,
        )
        replaced = jnp.where(
            panel_id == source_panel, own_factor, front_block[:, local_start : local_start + TILE]
        )
        front_block = front_block.at[:, local_start : local_start + TILE].set(replaced)
    upper_zone = (global_rows[:, None] < pivot_span) & (global_cols[None, :] >= pivot_span)
    return jnp.where(upper_zone, 0.0, front_block)


def solution(mesh):
    placed = (
        P("leaf", "panel", None),
        P("leaf", None, None),
        P("leaf", "panel"),
        P("leaf", None),
        P("leaf"),
    )
    return jax.shard_map(
        shards, mesh=mesh, in_specs=placed, out_specs=P("leaf", "panel"), check_vma=False
    )
```

profile of v0, /device:TPU:0, one launch (start us, length us, event | category | flops | bytes accessed | tf_op | source)
XLA Modules:
  0.0 964.4 jit_solution(7068307118465232745)
XLA Ops:
  6.5 11.5 %fusion.2 = f32[256,2048]{1,0:T(8,128)S(1)} fusion(bf16[1,2048,4096]{2,1,0:T(8,128)(2,1)} %param.23, f32[1,256,2048]{2,1,0:T(8,128)} %param.22, s32[]{:T(128)S(6)} %select_n.120), kind=kOutput, calls=%fused_computation.18 | convolution fusion | flops 4295491584 | bytes 23068676 | tf_op jit(solution)/shard_map/dot_general | solution.py:41
  23.2 5.2 reshape.226
  33.0 54.3 %all_to_all.15 = f32[256,8,512]{2,0,1:T(8,128)} all-to-all(f32[256,8,512]{2,0,1:T(8,128)S(1)} %copy.25), channel_id=1, replica_groups=mesh['leaf'=16,'panel'=8] {'panel'}, dimensions={1} | all-to-all | bytes 8388608 | tf_op jit(solution)/shard_map/all_to_all | solution.py:52
  87.4 5.5 copy.46
  92.8 5.5 fusion.118
  98.4 11.3 %copy.54 = f32[64,8,16,256]{3,1,2,0:T(8,128)} copy(f32[64,8,16,256]{3,2,1,0:T(8,128)S(1)} %bitcast.200) | data formatting | bytes 16777216
  110.9 85.6 %reduce-scatter.2.cloned.1.call-done = f32[256,512]{0,1:T(8,128)} async-done(((f32[4096,512]{0,1:T(8,128)}), f32[256,512]{0,1:T(8,128)}) %reduce-scatter.2.cloned.1.call-update) | async-done | bytes 524304 | tf_op jit(solution)/shard_map/reduce_scatter | solution.py:56
  198.4 60.0 %all-reduce.6.cloned.1.call-done = f32[256,256]{0,1:T(8,128)} async-done(((f32[256,256]{0,1:T(8,128)}), f32[256,256]{0,1:T(8,128)}) %all-reduce.6.cloned.1.call-update) | async-done | bytes 262160 | tf_op jit(solution)/shard_map/psum | solution.py:14
  259.5 57.1 %all-gather.5.cloned.1.call-done = f32[4096,256]{0,1:T(8,128)} async-done(((f32[256,256]{0,1:T(8,128)}), f32[4096,256]{0,1:T(8,128)}) %all-gather.5.cloned.1.call-update) | async-done | bytes 4194320 | tf_op jit(solution)/shard_map/all_gather | solution.py:73
  318.7 11.7 %cholesky.214 = f32[128,128]{1,0:T(8,128)S(1)} custom-call(f32[128,128]{1,0:T(8,128)S(1)} %cholesky.346), custom_call_target="Cholesky" | custom-call | tf_op jit(solution)/shard_map/jit(cholesky)/cholesky | solution.py:74
  330.4 9.8 %custom-call.23 = f32[1,128,128]{1,2,0:T(8,128)S(1)} custom-call(f32[1,128,128]{2,1,0:T(8,128)S(1)} %get-tuple-element.181), custom_call_target="InvertDiagBlocksLowerTriangular" | custom-call | tf_op jit(solution)/shard_map/jit(cholesky)/cholesky | solution.py:74
  340.7 11.7 %cholesky.231 = f32[128,128]{1,0:T(8,128)S(1)} custom-call(f32[128,128]{1,0:T(8,128)S(1)} %convolution_subtract_fusion.15), custom_call_target="Cholesky" | custom-call | tf_op jit(solution)/shard_map/jit(cholesky)/cholesky | solution.py:74
  358.8 20.1 %custom-call.24 = f32[2,128,128]{1,2,0:T(8,128)S(1)} custom-call(f32[2,128,128]{2,1,0:T(8,128)S(1)} %get-tuple-element.110), custom_call_target="InvertDiagBlocksLowerTriangular" | custom-call | tf_op jit(solution)/shard_map/triangular_solve/custom-call.0 | solution.py:18
  388.4 59.7 %all-reduce.8.cloned.1.call-done = f32[256,256]{0,1:T(8,128)} async-done(((f32[256,256]{0,1:T(8,128)}), f32[256,256]{0,1:T(8,128)}) %all-reduce.8.cloned.1.call-update) | async-done | bytes 262160 | tf_op jit(solution)/shard_map/psum | solution.py:14
  448.5 57.6 %all-gather.7.cloned.1.call-done = f32[4096,256]{0,1:T(8,128)} async-done(((f32[256,256]{0,1:T(8,128)}), f32[4096,256]{0,1:T(8,128)}) %all-gather.7.cloned.1.call-update) | async-done | bytes 4194320 | tf_op jit(solution)/shard_map/all_gather | solution.py:73
  508.3 11.7 %cholesky.248 = f32[128,128]{1,0:T(8,128)S(1)} custom-call(f32[128,128]{1,0:T(8,128)S(1)} %cholesky.349), custom_call_target="Cholesky" | custom-call | tf_op jit(solution)/shard_map/jit(cholesky)/cholesky | solution.py:74
  520.1 9.8 %custom-call.26 = f32[1,128,128]{1,2,0:T(8,128)S(1)} custom-call(f32[1,128,128]{2,1,0:T(8,128)S(1)} %get-tuple-element.177), custom_call_target="InvertDiagBlocksLowerTriangular" | custom-call | tf_op jit(solution)/shard_map/jit(cholesky)/cholesky | solution.py:74
  530.3 11.7 %cholesky.265 = f32[128,128]{1,0:T(8,128)S(1)} custom-call(f32[128,128]{1,0:T(8,128)S(1)} %convolution_subtract_fusion.14), custom_call_target="Cholesky" | custom-call | tf_op jit(solution)/shard_map/jit(cholesky)/cholesky | solution.py:74
  549.3 19.7 %custom-call.27 = f32[2,128,128]{1,2,0:T(8,128)S(1)} custom-call(f32[2,128,128]{2,1,0:T(8,128)S(1)} %get-tuple-element.112), custom_call_target="InvertDiagBlocksLowerTriangular" | custom-call | tf_op jit(solution)/shard_map/triangular_solve/custom-call.0 | solution.py:18
  577.8 59.7 %all-reduce.10.cloned.1.call-done = f32[256,256]{0,1:T(8,128)} async-done(((f32[256,256]{0,1:T(8,128)}), f32[256,256]{0,1:T(8,128)}) %all-reduce.10.cloned.1.call-update) | async-done | bytes 262160 | tf_op jit(solution)/shard_map/psum | solution.py:14
  637.9 57.7 %all-gather.9.cloned.1.call-done = f32[4096,256]{0,1:T(8,128)} async-done(((f32[256,256]{0,1:T(8,128)}), f32[4096,256]{0,1:T(8,128)}) %all-gather.9.cloned.1.call-update) | async-done | bytes 4194320 | tf_op jit(solution)/shard_map/all_gather | solution.py:73
  697.7 11.7 %cholesky.282 = f32[128,128]{1,0:T(8,128)S(1)} custom-call(f32[128,128]{1,0:T(8,128)S(1)} %cholesky.352), custom_call_target="Cholesky" | custom-call | tf_op jit(solution)/shard_map/jit(cholesky)/cholesky | solution.py:74
  709.5 9.8 %custom-call.29 = f32[1,128,128]{1,2,0:T(8,128)S(1)} custom-call(f32[1,128,128]{2,1,0:T(8,128)S(1)} %get-tuple-element.173), custom_call_target="InvertDiagBlocksLowerTriangular" | custom-call | tf_op jit(solution)/shard_map/jit(cholesky)/cholesky | solution.py:74
  719.8 11.7 %cholesky.299 = f32[128,128]{1,0:T(8,128)S(1)} custom-call(f32[128,128]{1,0:T(8,128)S(1)} %convolution_subtract_fusion.13), custom_call_target="Cholesky" | custom-call | tf_op jit(solution)/shard_map/jit(cholesky)/cholesky | solution.py:74
  734.3 4.6 while.22
  739.0 19.7 %custom-call.30 = f32[2,128,128]{1,2,0:T(8,128)S(1)} custom-call(f32[2,128,128]{2,1,0:T(8,128)S(1)} %get-tuple-element.114), custom_call_target="InvertDiagBlocksLowerTriangular" | custom-call | tf_op jit(solution)/shard_map/triangular_solve/custom-call.0 | solution.py:18
  768.4 59.5 %all-reduce.12.cloned.1.call-done = f32[256,256]{0,1:T(8,128)} async-done(((f32[256,256]{0,1:T(8,128)}), f32[256,256]{0,1:T(8,128)}) %all-reduce.12.cloned.1.call-update) | async-done | bytes 262160 | tf_op jit(solution)/shard_map/psum | solution.py:14
  828.0 58.0 %all-gather.11.cloned.1.call-done = f32[4096,256]{0,1:T(8,128)} async-done(((f32[256,256]{0,1:T(8,128)}), f32[4096,256]{0,1:T(8,128)}) %all-gather.11.cloned.1.call-update) | async-done | bytes 4194320 | tf_op jit(solution)/shard_map/all_gather | solution.py:73
  888.1 11.7 %cholesky.316 = f32[128,128]{1,0:T(8,128)S(1)} custom-call(f32[128,128]{1,0:T(8,128)S(1)} %cholesky.355), custom_call_target="Cholesky" | custom-call | tf_op jit(solution)/shard_map/jit(cholesky)/cholesky | solution.py:74
  899.9 9.8 %custom-call.32 = f32[1,128,128]{1,2,0:T(8,128)S(1)} custom-call(f32[1,128,128]{2,1,0:T(8,128)S(1)} %get-tuple-element.169), custom_call_target="InvertDiagBlocksLowerTriangular" | custom-call | tf_op jit(solution)/shard_map/jit(cholesky)/cholesky | solution.py:74
  910.2 11.7 %cholesky.333 = f32[128,128]{1,0:T(8,128)S(1)} custom-call(f32[128,128]{1,0:T(8,128)S(1)} %convolution_subtract_fusion.12), custom_call_target="Cholesky" | custom-call | tf_op jit(solution)/shard_map/jit(cholesky)/cholesky | solution.py:74
  928.8 19.7 %custom-call.33 = f32[2,128,128]{1,2,0:T(8,128)S(1)} custom-call(f32[2,128,128]{2,1,0:T(8,128)S(1)} %get-tuple-element.116), custom_call_target="InvertDiagBlocksLowerTriangular" | custom-call | tf_op jit(solution)/shard_map/triangular_solve/custom-call.0 | solution.py:18
  (202 shorter events, 95.5 us)
Async XLA Ops:
  6.5 190.0 %reduce-scatter.2.cloned.1.call-start = ((), (), s32[]{:S(2)}) async-start(), calls=%async_computation.2 | async-start | bytes 8912896 | tf_op jit(solution)/shard_map/reduce_scatter | solution.py:56
  18.0 1.6 copy-start.5
  109.7 1.0 copy-start.4
  109.7 148.7 %all-reduce.6.cloned.1.call-start = ((), (), s32[]{:S(2)}) async-start(), calls=%async_computation.3 | async-start | bytes 524288 | tf_op jit(solution)/shard_map/psum | solution.py:14
  198.3 118.2 %all-gather.5.cloned.1.call-start = ((), (), s32[]{:S(2)}) async-start(), calls=%async_computation.4 | async-start | bytes 4456448 | tf_op jit(solution)/shard_map/all_gather | solution.py:73
  258.4 120.5 %copy-start = (f32[256,256]{0,1:T(8,128)S(1)}, f32[256,256]{0,1:T(8,128)}, u32[]{:S(2)}) copy-start(f32[256,256]{0,1:T(8,128)} %all-reduce.6.cloned.1.call-done) | copy-start | bytes 786436
  258.4 189.7 %all-reduce.8.cloned.1.call-start = ((), (), s32[]{:S(2)}) async-start(), calls=%async_computation.5 | async-start | bytes 524288 | tf_op jit(solution)/shard_map/psum | solution.py:14
  388.4 117.8 %all-gather.7.cloned.1.call-start = ((), (), s32[]{:S(2)}) async-start(), calls=%async_computation.6 | async-start | bytes 4456448 | tf_op jit(solution)/shard_map/all_gather | solution.py:73
  448.2 120.8 %copy-start.2 = (f32[256,256]{0,1:T(8,128)S(1)}, f32[256,256]{0,1:T(8,128)}, u32[]{:S(2)}) copy-start(f32[256,256]{0,1:T(8,128)} %all-reduce.8.cloned.1.call-done) | copy-start | bytes 786436
  448.2 189.3 %all-reduce.10.cloned.1.call-start = ((), (), s32[]{:S(2)}) async-start(), calls=%async_computation.7 | async-start | bytes 524288 | tf_op jit(solution)/shard_map/psum | solution.py:14
  577.8 117.9 %all-gather.9.cloned.1.call-start = ((), (), s32[]{:S(2)}) async-start(), calls=%async_computation.8 | async-start | bytes 4456448 | tf_op jit(solution)/shard_map/all_gather | solution.py:73
  637.5 121.2 %copy-start.3 = (f32[256,256]{0,1:T(8,128)S(1)}, f32[256,256]{0,1:T(8,128)}, u32[]{:S(2)}) copy-start(f32[256,256]{0,1:T(8,128)} %all-reduce.10.cloned.1.call-done) | copy-start | bytes 786436
  637.5 190.3 %all-reduce.12.cloned.1.call-start = ((), (), s32[]{:S(2)}) async-start(), calls=%async_computation.9 | async-start | bytes 524288 | tf_op jit(solution)/shard_map/psum | solution.py:14
  768.1 117.9 %all-gather.11.cloned.1.call-start = ((), (), s32[]{:S(2)}) async-start(), calls=%async_computation.10 | async-start | bytes 4456448 | tf_op jit(solution)/shard_map/all_gather | solution.py:73
  827.8 120.6 %copy-start.1 = (f32[256,256]{0,1:T(8,128)S(1)}, f32[256,256]{0,1:T(8,128)}, u32[]{:S(2)}) copy-start(f32[256,256]{0,1:T(8,128)} %all-reduce.12.cloned.1.call-done) | copy-start | bytes 786436
Sparse Core Ops, SparseCore 0:
  109.8 86.6 reduce-scatter.1
  198.8 59.5 all-reduce.5
  260.5 55.9 all-gather.4
  388.5 59.6 all-reduce.7
  450.1 55.9 all-gather.6
  577.9 59.5 all-reduce.9
  639.6 55.9 all-gather.8
  768.3 59.5 all-reduce.11
  830.0 55.9 all-gather.10
where the time goes:
time: 972 us; the launch traced here: 964 us
  waiting for transfers between devices  555 us (57%)
  other arithmetic  228 us (23%)
  local copies, waits for them, and re-layouts  62 us (6%)
  blocking collectives  54.3 us (6%)
  matrix products  42.7 us (4%)
  between operations  20.3 us (2%)
    psum x4, waiting for transfers between devices, spread(): return lax.psum(jnp.where(mine, array, jnp.zeros_like(array)), axis)  239 us
    all_gather x4, waiting for transfers between devices, shards(): full_column = lax.all_gather(column, 'leaf', axis=0, tiled=True)  230 us
    another operation x27, other arithmetic, shards(): factor = jnp.linalg.cholesky(full_column[pivot_start:pivot_start + TILE])  138 us
    reduce_scatter x1, waiting for transfers between devices, shards(): lax.psum_scatter(jnp.einsum('ft,tbc->fbc', picked, column_tiles, precisio...  85.6 us
    another operation x9, other arithmetic, finish_rows(): lax.linalg.triangular_solve(factor, block, left_side=False, lower=True, t...  79.3 us
    all_to_all x1, blocking collectives, shards(): lax.all_to_all(placed, 'panel', split_axis=1, concat_axis=0, tiled=True)  54.3 us
  transfers between devices with their start and end apart: 9, of which 9 were waited for; matrix products, arithmetic and copies ran while one was open for 0% of the time, Pallas kernels for 0%

commit v1 on v0

--- a/solution.py
+++ b/solution.py
@@ -49,7 +49,21 @@
         "rtb,ft->rfb", update.reshape(child_rows, tiles_child, TILE), chosen, precision=highest
     )
     placed = placed.reshape(child_rows, panel_count, col_width)
-    moved_cols = lax.all_to_all(placed, "panel", split_axis=1, concat_axis=0, tiled=True)
+    reached = lax.axis_size("panel")
+    f_now = lax.axis_index("panel")
+    p_next, z2 = (reached, f_now)
+    passed = placed.shape[1] // p_next
+    oldest = list(placed.shape)
+    oldest[1] = passed
+    last = oldest[0]
+    oldest[0] = last * p_next
+    moved_cols = jnp.zeros(oldest, placed.dtype)
+    for tick in tuple(range(p_next)):
+        v_next = lax.dynamic_slice_in_dim(placed, (z2 ^ tick) * passed, passed, axis=1)
+        if tick:
+            main = tuple(((q, q ^ tick) for q in range(p_next)))
+            v_next = lax.ppermute(v_next, axis_name="panel", perm=main)
+        moved_cols = lax.dynamic_update_slice_in_dim(moved_cols, v_next, (z2 ^ tick) * last, axis=0)
     column_tiles = moved_cols.reshape(tiles_child, TILE, col_width)
     targets = jnp.arange(lax.axis_size("leaf") * height // TILE, dtype=jnp.int32)
     picked = ((mapped[None, :] == targets[:, None]) & live_tiles[None, :]).astype(jnp.float32)

time: 972 us -> 993 us (1.022)
  blocking collectives: 54.3 us -> 0 us
  local copies, waits for them, and re-layouts: 62 us -> 89.7 us
  waiting for transfers between devices: 555 us -> 578 us
  starting transfers between devices: 1.13 us -> 23.5 us
    all_to_all x1 -> x0, blocking collectives: 54.3 us -> none  [shards(): lax.all_to_all(placed, 'panel', split_axis=1, concat_axis=0, tiled=True)]
    ppermute x0 -> x7, waiting for transfers between devices: none -> 33.6 us  [shards(): v_next = lax.ppermute(v_next, axis_name='panel', perm=main)]
    dynamic_slice x0 -> x1, local copies, waits for them, and re-layouts: none -> 16.4 us  [shards(): lax.dynamic_slice_in_dim(placed, (z2 ^ tick) * passed, passed, axis=1)]
    dynamic_update_slice x0 -> x8, local copies, waits for them, and re-layouts: none -> 11.9 us  [shards(): lax.dynamic_update_slice_in_dim(moved_cols, v_next, (z2 ^ tick) * last, a...]
    all_gather x4, waiting for transfers between devices: 230 us -> 219 us  [shards(): full_column = lax.all_gather(column, 'leaf', axis=0, tiled=True)]
    psum x4, starting transfers between devices: 0.79 us -> 12.4 us  [spread(): return lax.psum(jnp.where(mine, array, jnp.zeros_like(array)), axis)]
    ppermute x0 -> x7, starting transfers between devices: none -> 10.7 us  [shards(): v_next = lax.ppermute(v_next, axis_name='panel', perm=main)]
  transfers between devices with their start and end apart: 9 -> 16, of which waited for: 9 -> 14; matrix products, arithmetic and copies ran while one was open for 0% -> 2% of each run, Pallas kernels for 0% -> 0%
where the time goes in v1:
time: 993 us; the launch traced here: 984 us
  waiting for transfers between devices  578 us (58%)
  other arithmetic  227 us (23%)
  local copies, waits for them, and re-layouts  89.7 us (9%)
  matrix products  42.7 us (4%)
  starting transfers between devices  23.5 us (2%)
  between operations  20.7 us (2%)
    psum x4, waiting for transfers between devices, spread(): return lax.psum(jnp.where(mine, array, jnp.zeros_like(array)), axis)  239 us
    all_gather x4, waiting for transfers between devices, shards(): full_column = lax.all_gather(column, 'leaf', axis=0, tiled=True)  219 us
    another operation x27, other arithmetic, shards(): factor = jnp.linalg.cholesky(full_column[pivot_start:pivot_start + TILE])  138 us
    reduce_scatter x1, waiting for transfers between devices, shards(): lax.psum_scatter(jnp.einsum('ft,tbc->fbc', picked, column_tiles, precisio...  86.8 us
    another operation x9, other arithmetic, finish_rows(): lax.linalg.triangular_solve(factor, block, left_side=False, lower=True, t...  78.8 us
    ppermute x7, waiting for transfers between devices, shards(): v_next = lax.ppermute(v_next, axis_name='panel', perm=main)  33.6 us
  transfers between devices with their start and end apart: 16, of which 14 were waited for; matrix products, arithmetic and copies ran while one was open for 2% of the time, Pallas kernels for 0%

profile of v1, /device:TPU:0, one launch (start us, length us, event | category | flops | bytes accessed | tf_op | source)
XLA Modules:
  0.0 983.6 jit_solution(4830645480521095008)
XLA Ops:
  6.5 11.5 %fusion.2 = f32[256,2048]{1,0:T(8,128)S(1)} fusion(bf16[1,2048,4096]{2,1,0:T(8,128)(2,1)} %param.23, f32[1,256,2048]{2,1,0:T(8,128)} %param.22, s32[]{:T(128)S(6)} %select_n.166), kind=kOutput, calls=%fused_computation.18 | convolution fusion | flops 4295491584 | bytes 23068676 | tf_op jit(solution)/shard_map/dot_general | solution.py:41
  28.4 16.4 %constant_dynamic-slice_fusion.4 = (f32[256,1,512]{2,1,0:T(1,128)S(1)}, f32[256,1,512]{2,1,0:T(1,128)S(1)}, f32[256,1,512]{2,1,0:T(1,128)S(1)}, f32[256,1,512]{2...) fusion(f32[256,8,512]{2,1,0:T(8,128)} %reshape.225, ...), kind=kLoop, calls=%fused_computation.192 | loop fusion | bytes 8388640 | tf_op jit(solution)/shard_map/dynamic_slice | solution.py:62
  64.7 6.3 collective-permute-done.2
  72.8 12.9 %collective-permute-done.3 = f32[256,1,512]{2,0,1:T(8,128)} collective-permute-done((f32[256,1,512]{2,0,1:T(8,128)S(1)}, f32[256,1,512]{2,0,1:T(8,128)}, u32[]{:S(2)}, u32[]{:S(2)}) %collective-permute-start.3) | collective-permute-done | bytes 524320 | tf_op jit(solution)/shard_map/ppermute | solution.py:65
  87.6 8.4 collective-permute-done.4
  116.5 11.3 %copy.69 = f32[64,8,16,256]{3,1,2,0:T(8,128)} copy(f32[64,8,16,256]{3,2,1,0:T(8,128)S(1)} %bitcast.197) | data formatting | bytes 16777216
  129.0 86.8 %reduce-scatter.2.cloned.1.call-done = f32[256,512]{0,1:T(8,128)} async-done(((f32[4096,512]{0,1:T(8,128)}), f32[256,512]{0,1:T(8,128)}) %reduce-scatter.2.cloned.1.call-update) | async-done | bytes 524304 | tf_op jit(solution)/shard_map/reduce_scatter | solution.py:70
  217.7 60.1 %all-reduce.6.cloned.1.call-done = f32[256,256]{0,1:T(8,128)} async-done(((f32[256,256]{0,1:T(8,128)}), f32[256,256]{0,1:T(8,128)}) %all-reduce.6.cloned.1.call-update) | async-done | bytes 262160 | tf_op jit(solution)/shard_map/psum | solution.py:14
  277.8 11.9 %all-reduce.8.cloned.1.call-start = ((), (), s32[]{:S(2)}) async-start(), calls=%async_computation.4 | async-start | bytes 524288 | tf_op jit(solution)/shard_map/psum | solution.py:14
  290.5 45.4 %all-gather.5.cloned.1.call-done = f32[4096,256]{0,1:T(8,128)} async-done(((f32[256,256]{0,1:T(8,128)}), f32[4096,256]{0,1:T(8,128)}) %all-gather.5.cloned.1.call-update) | async-done | bytes 4194320 | tf_op jit(solution)/shard_map/all_gather | solution.py:87
  338.1 11.7 %cholesky.214 = f32[128,128]{1,0:T(8,128)S(1)} custom-call(f32[128,128]{1,0:T(8,128)S(1)} %cholesky.346), custom_call_target="Cholesky" | custom-call | tf_op jit(solution)/shard_map/jit(cholesky)/cholesky | solution.py:88
  349.8 9.8 custom-call.23
  360.1 11.7 %cholesky.231 = f32[128,128]{1,0:T(8,128)S(1)} custom-call(f32[128,128]{1,0:T(8,128)S(1)} %convolution_subtract_fusion.15), custom_call_target="Cholesky" | custom-call | tf_op jit(solution)/shard_map/jit(cholesky)/cholesky | solution.py:88
  378.1 19.7 %custom-call.24 = f32[2,128,128]{1,2,0:T(8,128)S(1)} custom-call(f32[2,128,128]{2,1,0:T(8,128)S(1)} %get-tuple-element.110), custom_call_target="InvertDiagBlocksLowerTriangular" | custom-call | tf_op jit(solution)/shard_map/triangular_solve/custom-call.0 | solution.py:18
  407.3 59.7 %all-reduce.8.cloned.1.call-done = f32[256,256]{0,1:T(8,128)} async-done(((f32[256,256]{0,1:T(8,128)}), f32[256,256]{0,1:T(8,128)}) %all-reduce.8.cloned.1.call-update) | async-done | bytes 262160 | tf_op jit(solution)/shard_map/psum | solution.py:14
  467.5 57.6 %all-gather.7.cloned.1.call-done = f32[4096,256]{0,1:T(8,128)} async-done(((f32[256,256]{0,1:T(8,128)}), f32[4096,256]{0,1:T(8,128)}) %all-gather.7.cloned.1.call-update) | async-done | bytes 4194320 | tf_op jit(solution)/shard_map/all_gather | solution.py:87
  527.2 11.7 %cholesky.248 = f32[128,128]{1,0:T(8,128)S(1)} custom-call(f32[128,128]{1,0:T(8,128)S(1)} %cholesky.349), custom_call_target="Cholesky" | custom-call | tf_op jit(solution)/shard_map/jit(cholesky)/cholesky | solution.py:88
  538.9 9.8 custom-call.26
  549.2 11.7 %cholesky.265 = f32[128,128]{1,0:T(8,128)S(1)} custom-call(f32[128,128]{1,0:T(8,128)S(1)} %convolution_subtract_fusion.14), custom_call_target="Cholesky" | custom-call | tf_op jit(solution)/shard_map/jit(cholesky)/cholesky | solution.py:88
  568.2 19.7 %custom-call.27 = f32[2,128,128]{1,2,0:T(8,128)S(1)} custom-call(f32[2,128,128]{2,1,0:T(8,128)S(1)} %get-tuple-element.112), custom_call_target="InvertDiagBlocksLowerTriangular" | custom-call | tf_op jit(solution)/shard_map/triangular_solve/custom-call.0 | solution.py:18
  596.8 59.7 %all-reduce.10.cloned.1.call-done = f32[256,256]{0,1:T(8,128)} async-done(((f32[256,256]{0,1:T(8,128)}), f32[256,256]{0,1:T(8,128)}) %all-reduce.10.cloned.1.call-update) | async-done | bytes 262160 | tf_op jit(solution)/shard_map/psum | solution.py:14
  656.9 57.8 %all-gather.9.cloned.1.call-done = f32[4096,256]{0,1:T(8,128)} async-done(((f32[256,256]{0,1:T(8,128)}), f32[4096,256]{0,1:T(8,128)}) %all-gather.9.cloned.1.call-update) | async-done | bytes 4194320 | tf_op jit(solution)/shard_map/all_gather | solution.py:87
  716.8 11.7 %cholesky.282 = f32[128,128]{1,0:T(8,128)S(1)} custom-call(f32[128,128]{1,0:T(8,128)S(1)} %cholesky.352), custom_call_target="Cholesky" | custom-call | tf_op jit(solution)/shard_map/jit(cholesky)/cholesky | solution.py:88
  728.6 9.8 custom-call.29
  738.9 11.7 %cholesky.299 = f32[128,128]{1,0:T(8,128)S(1)} custom-call(f32[128,128]{1,0:T(8,128)S(1)} %convolution_subtract_fusion.13), custom_call_target="Cholesky" | custom-call | tf_op jit(solution)/shard_map/jit(cholesky)/cholesky | solution.py:88
  757.6 19.7 %custom-call.30 = f32[2,128,128]{1,2,0:T(8,128)S(1)} custom-call(f32[2,128,128]{2,1,0:T(8,128)S(1)} %get-tuple-element.114), custom_call_target="InvertDiagBlocksLowerTriangular" | custom-call | tf_op jit(solution)/shard_map/triangular_solve/custom-call.0 | solution.py:18
  787.1 59.5 %all-reduce.12.cloned.1.call-done = f32[256,256]{0,1:T(8,128)} async-done(((f32[256,256]{0,1:T(8,128)}), f32[256,256]{0,1:T(8,128)}) %all-reduce.12.cloned.1.call-update) | async-done | bytes 262160 | tf_op jit(solution)/shard_map/psum | solution.py:14
  846.7 58.0 %all-gather.11.cloned.1.call-done = f32[4096,256]{0,1:T(8,128)} async-done(((f32[256,256]{0,1:T(8,128)}), f32[4096,256]{0,1:T(8,128)}) %all-gather.11.cloned.1.call-update) | async-done | bytes 4194320 | tf_op jit(solution)/shard_map/all_gather | solution.py:87
  906.8 11.7 %cholesky.316 = f32[128,128]{1,0:T(8,128)S(1)} custom-call(f32[128,128]{1,0:T(8,128)S(1)} %cholesky.355), custom_call_target="Cholesky" | custom-call | tf_op jit(solution)/shard_map/jit(cholesky)/cholesky | solution.py:88
  918.6 9.8 custom-call.32
  928.9 11.7 %cholesky.333 = f32[128,128]{1,0:T(8,128)S(1)} custom-call(f32[128,128]{1,0:T(8,128)S(1)} %convolution_subtract_fusion.12), custom_call_target="Cholesky" | custom-call | tf_op jit(solution)/shard_map/jit(cholesky)/cholesky | solution.py:88
  947.6 19.7 %custom-call.33 = f32[2,128,128]{1,2,0:T(8,128)S(1)} custom-call(f32[2,128,128]{2,1,0:T(8,128)S(1)} %get-tuple-element.116), custom_call_target="InvertDiagBlocksLowerTriangular" | custom-call | tf_op jit(solution)/shard_map/triangular_solve/custom-call.0 | solution.py:18
  (231 shorter events, 144.0 us)
Async XLA Ops:
  6.5 209.3 %reduce-scatter.2.cloned.1.call-start = ((), (), s32[]{:S(2)}) async-start(), calls=%async_computation.1 | async-start | bytes 8912896 | tf_op jit(solution)/shard_map/reduce_scatter | solution.py:70
  18.0 1.6 copy-start.5
  45.6 9.9 %collective-permute-start = (f32[256,1,512]{2,0,1:T(8,128)}, f32[256,1,512]{2,0,1:T(8,128)}, u32[]{:S(2)}, u32[]{:S(2)}) collective-permute-start(f32[256,1,512]{2,0,1:T(8,128)} %copy.61), channel_id=1, source_target_pairs={{0,1},{1,0},{2,3},{3,2},{4,5},{5,4},{6,7},{7,6},{8,9},{9,8},{10,11... | collective-permute-start | bytes 1572872 | tf_op jit(solution)/shard_map/ppermute | solution.py:65
  45.7 15.0 %collective-permute-start.1 = (f32[256,1,512]{2,0,1:T(8,128)S(1)}, f32[256,1,512]{2,0,1:T(8,128)}, u32[]{:S(2)}, u32[]{:S(2)}) collective-permute-start(f32[256,1,512]{2,0,1:T(8,128)S(1)} %copy.62), channel_id=1, source_target_pairs={{0,2},{1,3},{2,0},{3,1},{4,6},{5,7},{6,4},{7,5},{8,10},{9,11},{10,... | collective-permute-start | bytes 1572872 | tf_op jit(solution)/shard_map/ppermute | solution.py:65
  47.5 23.5 %collective-permute-start.2 = (f32[256,1,512]{2,0,1:T(8,128)S(1)}, f32[256,1,512]{2,0,1:T(8,128)}, u32[]{:S(2)}, u32[]{:S(2)}) collective-permute-start(f32[256,1,512]{2,0,1:T(8,128)S(1)} %copy.63), channel_id=1, source_target_pairs={{0,3},{1,2},{2,1},{3,0},{4,7},{5,6},{6,5},{7,4},{8,11},{9,10},{10,... | collective-permute-start | bytes 1572872 | tf_op jit(solution)/shard_map/ppermute | solution.py:65
  47.7 38.0 %collective-permute-start.3 = (f32[256,1,512]{2,0,1:T(8,128)S(1)}, f32[256,1,512]{2,0,1:T(8,128)}, u32[]{:S(2)}, u32[]{:S(2)}) collective-permute-start(f32[256,1,512]{2,0,1:T(8,128)S(1)} %copy.64), channel_id=1, source_target_pairs={{0,4},{1,5},{2,6},{3,7},{4,0},{5,1},{6,2},{7,3},{8,12},{9,13},{10,... | collective-permute-start | bytes 1572872 | tf_op jit(solution)/shard_map/ppermute | solution.py:65
  51.2 44.9 %collective-permute-start.4 = (f32[256,1,512]{2,0,1:T(8,128)S(1)}, f32[256,1,512]{2,0,1:T(8,128)}, u32[]{:S(2)}, u32[]{:S(2)}) collective-permute-start(f32[256,1,512]{2,0,1:T(8,128)S(1)} %copy.65), channel_id=1, source_target_pairs={{0,5},{1,4},{2,7},{3,6},{4,1},{5,0},{6,3},{7,2},{8,13},{9,12},{10,... | collective-permute-start | bytes 1572872 | tf_op jit(solution)/shard_map/ppermute | solution.py:65
  55.5 42.4 %collective-permute-start.5 = (f32[256,1,512]{2,0,1:T(8,128)}, f32[256,1,512]{2,0,1:T(8,128)S(1)}, u32[]{:S(2)}, u32[]{:S(2)}) collective-permute-start(f32[256,1,512]{2,0,1:T(8,128)} %copy.66), channel_id=1, source_target_pairs={{0,6},{1,7},{2,4},{3,5},{4,2},{5,3},{6,0},{7,1},{8,14},{9,15},{10,... | collective-permute-start | bytes 1572872 | tf_op jit(solution)/shard_map/ppermute | solution.py:65
  60.6 44.0 %collective-permute-start.6 = (f32[256,1,512]{2,0,1:T(8,128)S(1)}, f32[256,1,512]{2,0,1:T(8,128)S(1)}, u32[]{:S(2)}, u32[]{:S(2)}) collective-permute-start(f32[256,1,512]{2,0,1:T(8,128)S(1)} %copy.67), channel_id=1, source_target_pairs={{0,7},{1,6},{2,5},{3,4},{4,3},{5,2},{6,1},{7,0},{8,15},{9,14},{10,... | collective-permute-start | bytes 1572872 | tf_op jit(solution)/shard_map/ppermute | solution.py:65
  127.8 1.0 copy-start.4
  127.8 150.0 %all-reduce.6.cloned.1.call-start = ((), (), s32[]{:S(2)}) async-start(), calls=%async_computation.2 | async-start | bytes 524288 | tf_op jit(solution)/shard_map/psum | solution.py:14
  217.7 118.3 %all-gather.5.cloned.1.call-start = ((), (), s32[]{:S(2)}) async-start(), calls=%async_computation.3 | async-start | bytes 4456448 | tf_op jit(solution)/shard_map/all_gather | solution.py:87
  277.8 120.0 %copy-start = (f32[256,256]{0,1:T(8,128)S(1)}, f32[256,256]{0,1:T(8,128)}, u32[]{:S(2)}) copy-start(f32[256,256]{0,1:T(8,128)} %all-reduce.6.cloned.1.call-done) | copy-start | bytes 786436
  277.8 189.2 %all-reduce.8.cloned.1.call-start = ((), (), s32[]{:S(2)}) async-start(), calls=%async_computation.4 | async-start | bytes 524288 | tf_op jit(solution)/shard_map/psum | solution.py:14
  407.3 117.8 %all-gather.7.cloned.1.call-start = ((), (), s32[]{:S(2)}) async-start(), calls=%async_computation.5 | async-start | bytes 4456448 | tf_op jit(solution)/shard_map/all_gather | solution.py:87
  467.1 120.8 %copy-start.2 = (f32[256,256]{0,1:T(8,128)S(1)}, f32[256,256]{0,1:T(8,128)}, u32[]{:S(2)}) copy-start(f32[256,256]{0,1:T(8,128)} %all-reduce.8.cloned.1.call-done) | copy-start | bytes 786436
  467.1 189.4 %all-reduce.10.cloned.1.call-start = ((), (), s32[]{:S(2)}) async-start(), calls=%async_computation.6 | async-start | bytes 524288 | tf_op jit(solution)/shard_map/psum | solution.py:14
  596.7 117.9 %all-gather.9.cloned.1.call-start = ((), (), s32[]{:S(2)}) async-start(), calls=%async_computation.7 | async-start | bytes 4456448 | tf_op jit(solution)/shard_map/all_gather | solution.py:87
  656.5 120.8 %copy-start.3 = (f32[256,256]{0,1:T(8,128)S(1)}, f32[256,256]{0,1:T(8,128)}, u32[]{:S(2)}) copy-start(f32[256,256]{0,1:T(8,128)} %all-reduce.10.cloned.1.call-done) | copy-start | bytes 786436
  656.6 190.0 %all-reduce.12.cloned.1.call-start = ((), (), s32[]{:S(2)}) async-start(), calls=%async_computation.8 | async-start | bytes 524288 | tf_op jit(solution)/shard_map/psum | solution.py:14
  786.8 117.9 %all-gather.11.cloned.1.call-start = ((), (), s32[]{:S(2)}) async-start(), calls=%async_computation.9 | async-start | bytes 4456448 | tf_op jit(solution)/shard_map/all_gather | solution.py:87
  846.6 120.7 %copy-start.1 = (f32[256,256]{0,1:T(8,128)S(1)}, f32[256,256]{0,1:T(8,128)}, u32[]{:S(2)}) copy-start(f32[256,256]{0,1:T(8,128)} %all-reduce.12.cloned.1.call-done) | copy-start | bytes 786436
Sparse Core Ops, SparseCore 0:
  127.9 87.8 reduce-scatter.1
  218.1 59.6 all-reduce.5
  279.9 55.9 all-gather.4
  407.4 59.6 all-reduce.7
  469.0 55.9 all-gather.6
  596.9 59.6 all-reduce.9
  658.6 55.9 all-gather.8
  786.9 59.6 all-reduce.11
  848.7 55.9 all-gather.10
